TPU v7x, 32 devices: a whole 2x2x4 slice. The times are simulated.
32 devices in a mesh: ang: 8 (over z, core), row: 4 (over y, x).
Axes of the slice: x: 2, y: 2, z: 4, core: 2. Of those that a mesh axis runs over, the one named last changes fastest.
Arguments:
- panels: bfloat16 [4, 32, 64, 2, 128], P('row', None, 'ang'), may hold values from -6 to 6
- panel_slot: int32 [4, 32], P('row'), may hold values from 0 to 15
- panel_cell: int32 [4, 32, 2], P('row'), may hold values from 0 to 15
- bloch_k: float32 [8, 2], replicated, may hold values from -3.140625 to 3.140625
- leaf_inverse: bfloat16 [8, 2, 8192, 256], P('ang', None, 'row'), may hold values from -0.25 to 0.25
- level_left: bfloat16 [8, 3, 2, 32, 8192], P('ang', None, None, None, 'row'), may hold values from -0.75 to 0.75
- level_right: bfloat16 [8, 3, 2, 32, 8192], P('ang', None, None, None, 'row'), may hold values from -0.125 to 0.125
- block_left: bfloat16 [8, 2, 32, 8192], P('ang', None, None, 'row'), may hold values from -0.75 to 0.75
- block_right: bfloat16 [8, 2, 32, 8192], P('ang', None, None, 'row'), may hold values from -0.09375 to 0.09375
- block_coupling: bfloat16 [8, 4, 2, 32, 128], P('ang', 'row'), may hold values from -0.375 to 0.375
- rank_count: int32 [8, 4], P('ang', 'row'), may hold values from 16 to 32
- quad_weight: float32 [8, 2], P('ang'), may hold values from -2 to 2
Outputs:
- response: float32 [64, 2, 8192], P('ang', None, 'row')
All inputs are finite; a program needn't handle non-finite values.
Results may differ from a plain program's by a relative error of at most 0.0045.
Values may be sent and summed in bfloat16 or wider, within the bound.
No kernel may reach another device: no remote copies, remote signals or barrier semaphores. Data moves between devices by JAX's collectives and lax.ppermute only.
A program may use at most 64 MiB of HBM per device.

v0:
```python
import jax
import jax.numpy as jnp
from jax import lax
from jax.sharding import PartitionSpec as P


def complex_product(form, left_real, left_imag, right_real, right_imag):

    def single(first, second):
        return jnp.einsum(form, first, second, preferred_element_type=jnp.float32)

    return (
        single(left_real, right_real) - single(left_imag, right_imag),
        single(left_real, right_imag) + single(left_imag, right_real),
    )


def assemble(phase_cosine, phase_sin, onehot, panel_group):
    coef_cos = phase_cosine[:, :, None] * onehot[None]
    coef_sin = phase_sin[:, :, None] * onehot[None]
    panel_real = panel_group[:, :, 0]
    panel_imag = panel_group[:, :, 1]

    def single(coefficient, entry_values):
        return jnp.einsum(
            "aqk,qsw->askw", coefficient, entry_values, preferred_element_type=jnp.float32
        )

    real_part = single(coef_cos, panel_real) + single(coef_sin, panel_imag)
    imag_part = single(coef_cos, panel_imag) - single(coef_sin, panel_real)
    stacked = jnp.stack([real_part, imag_part], 2)
    dims = stacked.shape
    return stacked.reshape(dims[0], dims[1], 2, dims[3] * dims[4]).astype(jnp.bfloat16)


def near_field(excite, leaf_block, right_factors, left_factors):
    source_count = excite.shape[0]
    row_count = excite.shape[2]
    leaf_width = leaf_block.shape[2]
    leaf_count = row_count // leaf_width
    rank_width = right_factors.shape[2]
    gathered_groups = excite.reshape(source_count, 2, leaf_count, leaf_width)
    real_part, imag_part = complex_product(
        "lwv,slv->slw",
        leaf_block[0].reshape(leaf_count, leaf_width, leaf_width),
        leaf_block[1].reshape(leaf_count, leaf_width, leaf_width),
        gathered_groups[:, 0],
        gathered_groups[:, 1],
    )
    real_part = real_part.reshape(source_count, row_count)
    imag_part = imag_part.reshape(source_count, row_count)
    for tree_level_index in range(right_factors.shape[0]):
        node_size = row_count // 2 ** (tree_level_index + 1)
        groups = row_count // node_size
        node_view = excite.reshape(source_count, 2, groups, node_size)
        right_real = right_factors[tree_level_index, 0].reshape(rank_width, groups, node_size)
        right_imag = right_factors[tree_level_index, 1].reshape(rank_width, groups, node_size)
        proj_real, proj_imag = complex_product(
            "rgm,sgm->sgr", right_real, right_imag, node_view[:, 0], node_view[:, 1]
        )
        projected = jnp.stack([proj_real, proj_imag], 1).astype(jnp.bfloat16)
        swapped = projected.reshape(source_count, 2, groups // 2, 2, rank_width)[
            :, :, :, ::-1
        ].reshape(source_count, 2, groups, rank_width)
        left_real = left_factors[tree_level_index, 0].reshape(rank_width, groups, node_size)
        left_imag = left_factors[tree_level_index, 1].reshape(rank_width, groups, node_size)
        add_real, add_imag = complex_product(
            "rgm,sgr->sgm", left_real, left_imag, swapped[:, 0], swapped[:, 1]
        )
        real_part = real_part + add_real.reshape(source_count, row_count)
        imag_part = imag_part + add_imag.reshape(source_count, row_count)
    return (real_part, imag_part)


def shards(
    panels,
    panel_slot,
    panel_cell,
    bloch_k,
    leaf_inverse,
    level_left,
    level_right,
    block_left,
    block_right,
    block_coupling,
    rank_count,
    quad_weight,
):
    local_angles = leaf_inverse.shape[0]
    row_count = leaf_inverse.shape[2]
    panel_width = panels.shape[4]
    slot_count = row_count // panel_width
    onehot = (panel_slot[0][:, None] == jnp.arange(slot_count, dtype=jnp.int32)[None, :]).astype(
        jnp.bfloat16
    )
    cell_float = panel_cell[0].astype(jnp.float32)
    own_wave = lax.dynamic_slice_in_dim(
        bloch_k, lax.axis_index("ang") * local_angles, local_angles, 0
    )
    theta = own_wave[:, 0:1] * cell_float[None, :, 0] + own_wave[:, 1:2] * cell_float[None, :, 1]
    own_cos = jnp.cos(theta).astype(jnp.bfloat16)
    own_sin = jnp.sin(theta).astype(jnp.bfloat16)
    excitation = assemble(
        own_cos, own_sin, onehot, lax.all_gather(panels, "ang", axis=2, tiled=True)[0]
    )
    rank_width = block_right.shape[2]
    rank_iota = jnp.arange(rank_width, dtype=jnp.int32)
    rank_masks = (rank_iota[None, :] < rank_count).astype(jnp.bfloat16)
    right_masked = block_right * rank_masks[:, None, :, None]
    left_masked = block_left * rank_masks[:, None, :, None]
    proj_real, proj_imag = complex_product(
        "arm,asm->asr",
        right_masked[:, 0],
        right_masked[:, 1],
        excitation[:, :, 0],
        excitation[:, :, 1],
    )
    projected = jnp.stack([proj_real, proj_imag], 2).astype(jnp.bfloat16)
    gathered = lax.all_gather(projected[:, None], "row", axis=1, tiled=True)
    number_of_blocks = gathered.shape[1]
    keep_other = (jnp.arange(number_of_blocks, dtype=jnp.int32) != lax.axis_index("row")).astype(
        jnp.bfloat16
    )
    gathered = gathered * keep_other[None, :, None, None, None]
    coupling = block_coupling[:, 0].reshape(
        local_angles, 2, rank_width, number_of_blocks, rank_width
    )
    coup_real, coup_imag = complex_product(
        "arjq,ajsq->asr", coupling[:, 0], coupling[:, 1], gathered[:, :, :, 0], gathered[:, :, :, 1]
    )
    coupled = jnp.stack([coup_real, coup_imag], 2).astype(jnp.bfloat16)
    excite_part = excitation[0]
    coupled_part = coupled[0]
    near_real, near_imag = near_field(excite_part, leaf_inverse[0], level_right[0], level_left[0])
    far_real, far_imag = complex_product(
        "rm,sr->sm", left_masked[0, 0], left_masked[0, 1], coupled_part[:, 0], coupled_part[:, 1]
    )
    field_real = near_real + far_real
    field_imag = near_imag + far_imag
    weight_real = quad_weight[0, 0]
    weight_imag = quad_weight[0, 1]
    summed = jnp.stack(
        [
            weight_real * field_real - weight_imag * field_imag,
            weight_real * field_imag + weight_imag * field_real,
        ],
        1,
    )
    return lax.psum_scatter(summed, "ang", scatter_dimension=0, tiled=True)


def solution(mesh):
    placed = (
        P("row", None, "ang", None, None),
        P("row", None),
        P("row", None, None),
        P(),
        P("ang", None, "row", None),
        P("ang", None, None, None, "row"),
        P("ang", None, None, None, "row"),
        P("ang", None, None, "row"),
        P("ang", None, None, "row"),
        P("ang", "row", None, None, None),
        P("ang", "row"),
        P("ang", None),
    )
    return jax.shard_map(
        shards, mesh=mesh, in_specs=placed, out_specs=P("ang", None, "row"), check_vma=False
    )
```

profile of v0, /device:TPU:0, one launch (start us, length us, event | category | flops | bytes accessed | tf_op | source)
XLA Modules:
  0.0 121.3 jit_solution(7901270127954322322)
XLA Ops:
  6.5 1.7 %copy.87 = bf16[1,32,8,2,128]{4,1,2,3,0:T(8,128)(2,1)} copy(bf16[1,32,8,2,128]{4,3,2,1,0:T(2,128)(2,1)} %param.12) | data formatting | bytes 262144 | tf_op args[0]
  9.0 1.3 %fusion.122 = (bf16[1,1,32,2048]{3,2,1,0:T(8,128)(2,1)S(1)}, bf16[1,1,32,2048]{3,2,1,0:T(8,128)(2,1)S(1)}, bf16[1,1,32,2048]{3,2,1,0:T(8,128)(2,1)S(1)}, bf16[1,...) fusion(bf16[3,2,32,2048]{3,2,1,0:T(8,128)(2,1)} %bitcast.282), kind=kLoop, calls=%fused_computation.173 | loop fusion | bytes 1572864 | tf_op jit(solution)/shard_map/slice | solution.py:57
  20.3 1.3 %convert_bitcast_fusion.1 = (bf16[32]{0:T(256)(128)(2,1)S(1)}, f32[32,1]{0,1:T(1,128)S(1)}) fusion(f32[32,2]{0,1:T(2,128)S(1)} %convert_bitcast_fusion, f32[]{:T(128)} %bitcast.4, f32[]{:T(128)} %bitcast.2), kind=kLoop, calls=%fused_computation.163 | loop fusion | flops 128 | bytes 456 | tf_op jit(solution)/shard_map/convert_element_type | solution.py:102
  23.2 1.7 %fusion.120 = (bf16[1,1,2048,256]{3,2,1,0:T(8,128)(2,1)S(1)}, bf16[1,1,2048,256]{3,2,1,0:T(8,128)(2,1)S(1)}) fusion(bf16[1,2,2048,256]{3,2,1,0:T(8,128)(2,1)} %param.16), kind=kLoop, calls=%fused_computation.171 | loop fusion | bytes 4194304 | tf_op jit(solution)/shard_map/slice | solution.py:46
  24.9 8.9 %all-gather.2.cloned.1.call-done = bf16[1,32,64,2,128]{4,1,2,3,0:T(8,128)(2,1)} async-done(((bf16[1,32,8,2,128]{4,1,2,3,0:T(8,128)(2,1)}), bf16[1,32,64,2,128]{4,1,2,3,0:T(8,128)(2,1)}) %all-gather.2.cloned.1.call-update) | async-done | bytes 1048592 | tf_op jit(solution)/shard_map/all_gather | solution.py:104
  33.9 1.3 %fusion.28 = f32[16,64,128]{2,0,1:T(8,128)S(1)} fusion(bf16[32,64,2,128]{3,0,1,2:T(8,128)(2,1)} %bitcast.250, s32[32]{0:T(128)S(1)} %bitcast.298, bf16[32]{0:T(256)(128)(2,1)S(1)} %convert_bitcast_fusion.2), kind=kOutput, calls=%fused_computation.57 | convolution fusion | flops 8389632 | bytes 1048768 | tf_op jit(solution)/shard_map/aqk,qsw->askw/dot_general | solution.py:25
  35.2 2.1 %fusion.29 = f32[16,64,128]{2,0,1:T(8,128)} fusion(bf16[32,64,2,128]{3,0,1,2:T(8,128)(2,1)} %bitcast.251, s32[32]{0:T(128)S(1)} %bitcast.299, bf16[32]{0:T(256)(128)(2,1)S(1)} %convert_bitcast_fusion.2), kind=kOutput, calls=%fused_computation.58 | convolution fusion | flops 8389632 | bytes 1048768 | tf_op jit(solution)/shard_map/aqk,qsw->askw/dot_general | solution.py:25
  39.0 2.0 %fusion.11 = bf16[16,64,128]{2,0,1:T(8,128)(2,1)} fusion(f32[16,64,128]{2,0,1:T(8,128)} %fusion.29, bf16[32,64,2,128]{3,0,1,2:T(8,128)(2,1)S(1)} %bitcast.253, s32[32]{0:T(128)S(1)} %bitcast.301, bf16[32]{0:T(256)(128)(2,1)S(1)} %get-tuple-element.5), kind=kOutput, calls=%fused_computation.23 | convolution fusion | flops 8651776 | bytes 1311744 | tf_op jit(solution)/shard_map/aqk,qsw->askw/dot_general | solution.py:25
  41.0 1.1 squeeze.95
  42.1 1.7 %squeeze.90 = bf16[64,2,1024]{2,1,0:T(2,128)(2,1)} reshape(bf16[1,64,16,128]{3,2,1,0:T(8,128)(2,1)} %bitcast.260) | data formatting | bytes 524288 | tf_op jit(solution)/shard_map/squeeze | solution.py:59
  43.9 1.2 fusion.44
  45.1 1.1 fusion.40
  50.2 1.1 fusion.30
  51.3 1.1 fusion.27
  52.4 1.1 fusion.26
  53.6 8.2 %all_gather.7 = bf16[1,4,64,2,32]{2,4,3,0,1:T(8,128)(2,1)S(1)} all-gather(bf16[1,1,64,2,32]{2,4,3,0,1:T(8,128)(2,1)S(1)} %maximum_bitcast_fusion), channel_id=1, replica_groups=mesh['ang'=8,'row'=4] {'row'}, dimensions={1}, use_global_device_ids=true | all-gather | bytes 40960 | tf_op jit(solution)/shard_map/all_gather | solution.py:119
  61.8 1.5 %convolution_bitcast_fusion = f32[64,32]{0,1:T(8,128)} fusion(bf16[1,1,32,4,32]{4,3,2,1,0:T(4,128)(2,1)} %get-tuple-element.24, bf16[1,4,64,2,32]{2,4,1,3,0:T(8,128)(2,1)S(1)} %copy_multiply_fusion), kind=kOutput, calls=%fused_computation.36 | convolution fusion | flops 524288 | bytes 49152 | tf_op jit(solution)/shard_map/arjq,ajsq->asr/dot_general | solution.py:10
  63.3 1.5 %convolution_bitcast_fusion.2 = f32[64,32]{0,1:T(8,128)} fusion(bf16[1,1,32,4,32]{4,3,2,1,0:T(4,128)(2,1)} %get-tuple-element.24, bf16[1,4,64,2,32]{2,4,1,3,0:T(8,128)(2,1)S(1)} %copy_multiply_fusion), kind=kOutput, calls=%fused_computation.38 | convolution fusion | flops 524288 | bytes 49152 | tf_op jit(solution)/shard_map/arjq,ajsq->asr/dot_general | solution.py:10
  66.0 1.1 fusion.54
  69.8 1.2 %fusion.62 = f32[8,64,256]{2,1,0:T(8,128)} fusion(bf16[8,256,256]{2,1,0:T(8,128)(2,1)S(1)} %bitcast.246, bf16[64,8,256]{2,1,0:T(8,128)(2,1)S(1)} %squeeze.86), kind=kOutput, calls=%fused_computation.91 | convolution fusion | flops 67108864 | bytes 1835008 | tf_op jit(solution)/shard_map/lwv,slv->slw/dot_general | solution.py:10
  71.0 1.2 %fusion.52 = f32[8,64,256]{2,1,0:T(8,128)} fusion(bf16[8,256,256]{2,1,0:T(8,128)(2,1)S(1)} %bitcast.247, bf16[64,8,256]{2,1,0:T(8,128)(2,1)S(1)} %squeeze.87), kind=kOutput, calls=%fused_computation.81 | convolution fusion | flops 67108864 | bytes 1835008 | tf_op jit(solution)/shard_map/lwv,slv->slw/dot_general | solution.py:10
  78.9 1.7 %subtract_bitcast_fusion = (f32[64,1,2048]{2,0,1:T(8,128)S(1)}, f32[64,1,2048]{2,0,1:T(8,128)S(1)}) fusion(f32[64,2048]{1,0:T(8,128)S(1)} %fusion, f32[]{:T(128)} %bitcast.66, f32[]{:T(128)} %bitcast, f32[64,2048]{1,0:T(8,128)S(1)} %fusion.64, bf16[64,32]{0,1:T(8,128)(2,1)S(1)} %fusion.23, bf16[1,2,32,2048]{3,2,1,0:T(8,128)(2,1)S(1)} %copy-done.3, ...), kind=kOutput, calls=%fused_computation.56 | convolution fusion | flops 9830400 | bytes 4333576 | tf_op jit(solution)/shard_map/rm,sr->sm/dot_general | solution.py:10
  81.7 31.1 %reduce-scatter.2.cloned.1.call-done = f32[8,2,2048]{2,0,1:T(8,128)} async-done(((f32[64,2,2048]{2,0,1:T(8,128)}), f32[8,2,2048]{2,0,1:T(8,128)}) %reduce-scatter.2.cloned.1.call-update) | async-done | bytes 131088 | tf_op jit(solution)/shard_map/reduce_scatter | solution.py:149
  112.8 1.7 %copy.140 = f32[8,2,2048]{2,1,0:T(2,128)} copy(f32[8,2,2048]{2,0,1:T(8,128)} %reduce-scatter.2.cloned.1.call-done) | data formatting | bytes 262144 | tf_op jit(solution)/shard_map/reduce_scatter | solution.py:149
  (160 shorter events, 28.5 us)
Async XLA Ops:
  6.5 5.2 %copy-start = (f32[8,2]{0,1:T(2,128)S(1)}, f32[8,2]{0,1:T(2,128)}, u32[]{:S(2)}) copy-start(f32[8,2]{0,1:T(2,128)} %param.15) | copy-start | bytes 196
  6.5 3.7 %copy-start.18 = (bf16[1,3,2,32,2048]{4,3,2,1,0:T(8,128)(2,1)S(1)}, bf16[1,3,2,32,2048]{4,3,2,1,0:T(8,128)(2,1)}, u32[]{:S(2)}) copy-start(bf16[1,3,2,32,2048]{4,3,2,1,0:T(8,128)(2,1)} %param.17) | copy-start | bytes 2359300
  6.5 4.5 %copy-start.40 = (f32[1,2]{1,0:T(1,128)S(1)}, f32[1,2]{1,0:T(1,128)}, u32[]{:S(2)}) copy-start(f32[1,2]{1,0:T(1,128)} %param.23) | copy-start | bytes 28
  6.5 27.3 %all-gather.2.cloned.1.call-start = ((), (), s32[]{:S(2)}) async-start(), calls=%async_computation.1 | async-start | bytes 1179648 | tf_op jit(solution)/shard_map/all_gather | solution.py:104
  8.2 104.6 %reduce-scatter.2.cloned.1.call-start = ((), (), s32[]{:S(2)}) async-start(), calls=%async_computation.2 | async-start | bytes 1179648 | tf_op jit(solution)/shard_map/reduce_scatter | solution.py:149
  10.2 9.4 %copy-start.38 = (bf16[1,1,2,32,128]{4,3,2,1,0:T(8,128)(2,1)S(1)}, bf16[1,1,2,32,128]{4,3,2,1,0:T(8,128)(2,1)}, u32[]{:S(2)}) copy-start(bf16[1,1,2,32,128]{4,3,2,1,0:T(8,128)(2,1)} %param.21) | copy-start | bytes 49156
  10.3 12.0 %copy-start.29 = (bf16[1,2,32,2048]{3,2,1,0:T(8,128)(2,1)S(1)}, bf16[1,2,32,2048]{3,2,1,0:T(8,128)(2,1)}, u32[]{:S(2)}) copy-start(bf16[1,2,32,2048]{3,2,1,0:T(8,128)(2,1)} %param.19) | copy-start | bytes 786436
  10.3 12.0 %copy-start.30 = (bf16[1,2,32,2048]{3,2,1,0:T(8,128)(2,1)S(1)}, bf16[1,2,32,2048]{3,2,1,0:T(8,128)(2,1)}, u32[]{:S(2)}) copy-start(bf16[1,2,32,2048]{3,2,1,0:T(8,128)(2,1)} %param.20) | copy-start | bytes 786436
  23.2 10.6 %copy-start.39 = (s32[1,32]{1,0:T(1,128)S(1)}, s32[1,32]{1,0:T(1,128)}, u32[]{:S(2)}) copy-start(s32[1,32]{1,0:T(1,128)} %param.13) | copy-start | bytes 388
  33.8 3.4 %copy-start.1 = (bf16[1,32,64,2,128]{4,1,2,3,0:T(8,128)(2,1)S(1)}, bf16[1,32,64,2,128]{4,1,2,3,0:T(8,128)(2,1)}, u32[]{:S(2)}) copy-start(bf16[1,32,64,2,128]{4,1,2,3,0:T(8,128)(2,1)} %all-gather.2.cloned.1.call-done) | copy-start | bytes 3145732
  41.0 5.2 %copy-start.35 = (bf16[32,4,512]{2,1,0:T(4,128)(2,1)S(1)}, bf16[32,4,512]{2,1,0:T(4,128)(2,1)}, u32[]{:S(2)}) copy-start(bf16[32,4,512]{2,1,0:T(4,128)(2,1)} %reshape_squeeze.56) | copy-start | bytes 393220
  41.0 5.4 %copy-start.28 = (bf16[64,4,512]{2,1,0:T(4,128)(2,1)S(1)}, bf16[64,4,512]{2,1,0:T(4,128)(2,1)}, u32[]{:S(2)}) copy-start(bf16[64,4,512]{2,1,0:T(4,128)(2,1)} %squeeze.94) | copy-start | bytes 786436
  41.0 5.7 %copy-start.15 = (bf16[32,4,512]{2,1,0:T(4,128)(2,1)S(1)}, bf16[32,4,512]{2,1,0:T(4,128)(2,1)}, u32[]{:S(2)}) copy-start(bf16[32,4,512]{2,1,0:T(4,128)(2,1)} %reshape_squeeze.57) | copy-start | bytes 393220
  43.9 5.1 %copy-start.2 = (bf16[16,64,128]{2,0,1:T(8,128)(2,1)S(1)}, bf16[16,64,128]{2,0,1:T(8,128)(2,1)}, u32[]{:S(2)}) copy-start(bf16[16,64,128]{2,0,1:T(8,128)(2,1)} %fusion.11) | copy-start | bytes 786436
  46.7 2.2 %copy-start.21 = (bf16[64,2,2,2,32]{0,4,3,2,1:T(8,128)(2,1)}, bf16[64,2,2,2,32]{0,4,3,2,1:T(8,128)(2,1)S(1)}, u32[]{:S(2)}) copy-start(bf16[64,2,2,2,32]{0,4,3,2,1:T(8,128)(2,1)S(1)} %rev.7) | copy-start | bytes 98308
  48.9 18.2 %copy-start.14 = (bf16[4,8,8,256]{3,2,1,0:T(8,128)(2,1)S(1)}, bf16[4,8,8,256]{3,2,1,0:T(8,128)(2,1)}, u32[]{:S(2)}) copy-start(bf16[4,8,8,256]{3,2,1,0:T(8,128)(2,1)} %copy.152) | copy-start | bytes 393220
  51.3 16.4 %copy-start.13 = (bf16[4,8,8,256]{3,2,1,0:T(8,128)(2,1)S(1)}, bf16[4,8,8,256]{3,2,1,0:T(8,128)(2,1)}, u32[]{:S(2)}) copy-start(bf16[4,8,8,256]{3,2,1,0:T(8,128)(2,1)} %copy.153) | copy-start | bytes 393220
  61.8 8.0 %copy-start.19 = (bf16[1,4,64,2,32]{2,4,1,3,0:T(8,128)(2,1)}, bf16[1,4,64,2,32]{2,4,1,3,0:T(8,128)(2,1)S(1)}, u32[]{:S(2)}) copy-start(bf16[1,4,64,2,32]{2,4,1,3,0:T(8,128)(2,1)S(1)} %copy_multiply_fusion) | copy-start | bytes 98308
  67.6 4.7 %copy-start.16 = (bf16[64,2,4,2,32]{0,4,3,2,1:T(8,128)(2,1)}, bf16[64,2,4,2,32]{0,4,3,2,1:T(8,128)(2,1)S(1)}, u32[]{:S(2)}) copy-start(bf16[64,2,4,2,32]{0,4,3,2,1:T(8,128)(2,1)S(1)} %rev.8) | copy-start | bytes 196612
  68.7 3.6 %copy-start.5 = (f32[4,64,512]{2,1,0:T(8,128)S(1)}, f32[4,64,512]{2,1,0:T(8,128)}, u32[]{:S(2)}) copy-start(f32[4,64,512]{2,1,0:T(8,128)} %fusion.78) | copy-start | bytes 1572868
  68.7 3.6 %copy-start.11 = (bf16[32,4,512]{2,1,0:T(4,128)(2,1)S(1)}, bf16[32,4,512]{2,1,0:T(4,128)(2,1)}, u32[]{:S(2)}) copy-start(bf16[32,4,512]{2,1,0:T(4,128)(2,1)} %reshape_squeeze.58) | copy-start | bytes 393220
  68.7 3.6 %copy-start.22 = (bf16[64,2,2,2,32]{0,4,3,2,1:T(8,128)(2,1)S(1)}, bf16[64,2,2,2,32]{0,4,3,2,1:T(8,128)(2,1)}, u32[]{:S(2)}) copy-start(bf16[64,2,2,2,32]{0,4,3,2,1:T(8,128)(2,1)} %copy-done.21) | copy-start | bytes 98308
  71.0 1.6 %copy-start.34 = (bf16[32,2,1024]{2,1,0:T(2,128)(2,1)S(1)}, bf16[32,2,1024]{2,1,0:T(2,128)(2,1)}, u32[]{:S(2)}) copy-start(bf16[32,2,1024]{2,1,0:T(2,128)(2,1)} %reshape_squeeze.51) | copy-start | bytes 393220
  71.0 1.8 %copy-start.27 = (bf16[64,2,1024]{2,1,0:T(2,128)(2,1)S(1)}, bf16[64,2,1024]{2,1,0:T(2,128)(2,1)}, u32[]{:S(2)}) copy-start(bf16[64,2,1024]{2,1,0:T(2,128)(2,1)} %squeeze.90) | copy-start | bytes 786436
  (19 other events, 22.2 us)
Sparse Core Ops, SparseCore 0:
  9.0 24.8 all-gather.1
  81.8 30.9 reduce-scatter.1
where the time goes:
time: 122 us; the launch traced here: 121 us
  waiting for transfers between devices  40.1 us (33%)
  matrix products  31.9 us (26%)
  local copies, waits for them, and re-layouts  22.2 us (18%)
  between operations  14.7 us (12%)
  blocking collectives  8.16 us (7%)
  other arithmetic  4.16 us (3%)
    reduce_scatter x1, waiting for transfers between devices, shards(): return lax.psum_scatter(summed, 'ang', scatter_dimension=0, tiled=True)  31.1 us
    dot_general x40, matrix products, single(): return jnp.einsum(form, first, second, preferred_element_type=jnp.float32)  26.3 us
    all_gather x1, waiting for transfers between devices, shards(): lax.all_gather(panels, 'ang', axis=2, tiled=True)[0]  8.91 us
    all_gather x1, blocking collectives, shards(): gathered = lax.all_gather(projected[:, None], 'row', axis=1, tiled=True)  8.16 us
    dot_general x4, matrix products, single(): jnp.einsum('aqk,qsw->askw', coefficient, entry_values, preferred_element_...  5.57 us
    unnamed x87, local copies, waits for them, and re-layouts  5.45 us
    squeeze x2, local copies, waits for them, and re-layouts, near_field(): node_view[:, 1]  2.85 us
  transfers between devices with their start and end apart: 2, of which 2 were waited for; matrix products, arithmetic and copies ran while one was open for 13% of the time, Pallas kernels for 0%

commit v1 on v0

--- a/solution.py
+++ b/solution.py
@@ -2,6 +2,27 @@
 import jax.numpy as jnp
 from jax import lax
 from jax.sharding import PartitionSpec as P
+
+
+def collect(array, axis, dim):
+    length, index, width = (lax.axis_size(axis), lax.axis_index(axis), array.shape[dim])
+    right = [(i, (i + 1) % length) for i in range(length)]
+    left = [(i, (i - 1) % length) for i in range(length)]
+    filled = jnp.zeros((*array.shape[:dim], length * width, *array.shape[dim + 1 :]), array.dtype)
+    filled = lax.dynamic_update_slice_in_dim(filled, array, index * width, axis=dim)
+    from_left = from_right = array
+    half = length // 2
+    for lap in range(1, half + 1):
+        from_left = lax.ppermute(from_left, axis, right)
+        filled = lax.dynamic_update_slice_in_dim(
+            filled, from_left, (index - lap) % length * width, axis=dim
+        )
+        if lap < length - half:
+            from_right = lax.ppermute(from_right, axis, left)
+            filled = lax.dynamic_update_slice_in_dim(
+                filled, from_right, (index + lap) % length * width, axis=dim
+            )
+    return filled
 
 
 def complex_product(form, left_real, left_imag, right_real, right_imag):
@@ -100,9 +121,7 @@
     theta = own_wave[:, 0:1] * cell_float[None, :, 0] + own_wave[:, 1:2] * cell_float[None, :, 1]
     own_cos = jnp.cos(theta).astype(jnp.bfloat16)
     own_sin = jnp.sin(theta).astype(jnp.bfloat16)
-    excitation = assemble(
-        own_cos, own_sin, onehot, lax.all_gather(panels, "ang", axis=2, tiled=True)[0]
-    )
+    excitation = assemble(own_cos, own_sin, onehot, collect(panels, "ang", 2)[0])
     rank_width = block_right.shape[2]
     rank_iota = jnp.arange(rank_width, dtype=jnp.int32)
     rank_masks = (rank_iota[None, :] < rank_count).astype(jnp.bfloat16)

time: 122 us -> 150 us (1.23)
  local copies, waits for them, and re-layouts: 22.2 us -> 38.7 us
  starting transfers between devices: 0.04 us -> 11.6 us
  matrix products: 31.9 us -> 28.6 us
  other arithmetic: 4.16 us -> 6.37 us
    ppermute x0 -> x7, starting transfers between devices: none -> 11.6 us  [the longest x3 11.2 us: collect(): from_right = lax.ppermute(from_right, axis, left)]
    ppermute x0 -> x7, waiting for transfers between devices: none -> 10.8 us  [the longest x4 10.5 us: collect(): from_left = lax.ppermute(from_left, axis, right)]
    all_gather x1 -> x0, waiting for transfers between devices: 8.91 us -> none  [shards(): lax.all_gather(panels, 'ang', axis=2, tiled=True)[0]]
    dynamic_update_slice x0 -> x8, local copies, waits for them, and re-layouts: none -> 2.91 us  [the longest x4 0.98 us: collect(): lax.dynamic_update_slice_in_dim(filled, from_left, (index - lap) % length...]
    unnamed x87 -> x75, local copies, waits for them, and re-layouts: 5.45 us -> 8.13 us
    dot_general x4, matrix products: 5.57 us -> 3.39 us  [single(): jnp.einsum('aqk,qsw->askw', coefficient, entry_values, preferred_element_...]
    another operation x2, local copies, waits for them, and re-layouts: 1.45 us -> 3.27 us  [near_field(): right_factors[tree_level_index, 0].reshape(rank_width, groups, node_size)]
    another operation x2, local copies, waits for them, and re-layouts: 1.45 us -> 3.26 us  [near_field(): left_factors[tree_level_index, 0].reshape(rank_width, groups, node_size)]
  transfers between devices with their start and end apart: 2 -> 8, of which waited for: 2 -> 5; matrix products, arithmetic and copies ran while one was open for 13% -> 20% of each run, Pallas kernels for 0% -> 0%
where the time goes in v1:
time: 150 us; the launch traced here: 149 us
  waiting for transfers between devices  40.6 us (27%)
  local copies, waits for them, and re-layouts  38.7 us (26%)
  matrix products  28.6 us (19%)
  between operations  14.6 us (10%)
  starting transfers between devices  11.6 us (8%)
  blocking collectives  8.87 us (6%)
  other arithmetic  6.37 us (4%)
    reduce_scatter x1, waiting for transfers between devices, shards(): return lax.psum_scatter(summed, 'ang', scatter_dimension=0, tiled=True)  29.8 us
    dot_general x40, matrix products, single(): return jnp.einsum(form, first, second, preferred_element_type=jnp.float32)  25.3 us
    ppermute x3, starting transfers between devices, collect(): from_right = lax.ppermute(from_right, axis, left)  11.2 us
    ppermute x4, waiting for transfers between devices, collect(): from_left = lax.ppermute(from_left, axis, right)  10.5 us
    all_gather x1, blocking collectives, shards(): gathered = lax.all_gather(projected[:, None], 'row', axis=1, tiled=True)  8.87 us
    unnamed x75, local copies, waits for them, and re-layouts  8.13 us
    squeeze x2, local copies, waits for them, and re-layouts, near_field(): node_view[:, 1]  3.5 us
    dot_general x4, matrix products, single(): jnp.einsum('aqk,qsw->askw', coefficient, entry_values, preferred_element_...  3.39 us
  transfers between devices with their start and end apart: 8, of which 5 were waited for; matrix products, arithmetic and copies ran while one was open for 20% of the time, Pallas kernels for 0%

profile of v1, /device:TPU:0, one launch (start us, length us, event | category | flops | bytes accessed | tf_op | source)
XLA Modules:
  0.0 149.5 jit_solution(15339125981658758820)
XLA Ops:
  6.5 1.7 %copy.91 = bf16[1,32,8,2,128]{4,1,2,3,0:T(8,128)(2,1)} copy(bf16[1,32,8,2,128]{4,3,2,1,0:T(2,128)(2,1)} %param.12) | data formatting | bytes 262144 | tf_op args[0]
  8.7 4.0 %collective-permute-start.1 = (bf16[1,32,8,2,128]{4,1,2,3,0:T(8,128)(2,1)}, bf16[1,32,8,2,128]{4,1,2,3,0:T(8,128)(2,1)}, u32[]{:S(2)}, u32[]{:S(2)}) collective-permute-start(bf16[1,32,8,2,128]{4,1,2,3,0:T(8,128)(2,1)} %copy.91), channel_id=1, source_target_pairs={{0,28},{4,0},{8,4},{12,8},{16,12},{20,16},{24,20},{28,24},{1,29},{... | collective-permute-start | bytes 393224 | tf_op jit(solution)/shard_map/ppermute | solution.py:21
  15.4 2.0 %fusion.122 = (bf16[1,1,32,2048]{3,2,1,0:T(8,128)(2,1)}, bf16[1,1,32,2048]{3,2,1,0:T(8,128)(2,1)S(1)}, bf16[1,1,32,2048]{3,2,1,0:T(8,128)(2,1)S(1)}, bf16[1,1,32...) fusion(bf16[3,2,32,2048]{3,2,1,0:T(8,128)(2,1)} %bitcast.289), kind=kLoop, calls=%fused_computation.181 | loop fusion | bytes 1572864 | tf_op jit(solution)/shard_map/slice | solution.py:78
  20.9 1.9 %broadcast_multiply_fusion = (bf16[1,2,32,2048]{3,2,1,0:T(8,128)(2,1)}, bf16[1,2,32,2048]{3,2,1,0:T(8,128)(2,1)}) fusion(bf16[1,2,32,2048]{3,2,1,0:T(8,128)(2,1)} %param.19, bf16[32]{0:T(256)(128)(2,1)S(1)} %compare_convert_fusion.1, bf16[1,2,32,2048]{3,2,1,0:T(8,128)(2,1)} %param.20), kind=kLoop, calls=%fused_computation.106 | loop fusion | flops 262144 | bytes 1048640 | tf_op jit(solution)/shard_map/mul | solution.py:129
  23.4 1.6 %reshape_squeeze.51 = bf16[32,2,1024]{2,1,0:T(2,128)(2,1)} reshape(bf16[1,1,32,2048]{3,2,1,0:T(8,128)(2,1)} %get-tuple-element.22) | data formatting | bytes 262144 | tf_op jit(solution)/shard_map/reshape;squeeze | solution.py:77
  25.1 1.6 %reshape_squeeze.52 = bf16[32,2,1024]{2,1,0:T(2,128)(2,1)} reshape(bf16[1,1,32,2048]{3,2,1,0:T(8,128)(2,1)} %get-tuple-element.17) | data formatting | bytes 262144 | tf_op jit(solution)/shard_map/reshape;squeeze | solution.py:78
  26.7 1.6 %reshape_squeeze.53 = bf16[32,2,1024]{2,1,0:T(2,128)(2,1)} reshape(bf16[1,1,32,2048]{3,2,1,0:T(8,128)(2,1)} %get-tuple-element.16) | data formatting | bytes 262144 | tf_op jit(solution)/shard_map/reshape;squeeze | solution.py:86
  28.3 1.6 %reshape_squeeze.54 = bf16[32,2,1024]{2,1,0:T(2,128)(2,1)} reshape(bf16[1,1,32,2048]{3,2,1,0:T(8,128)(2,1)} %get-tuple-element.11) | data formatting | bytes 262144 | tf_op jit(solution)/shard_map/reshape;squeeze | solution.py:87
  30.0 1.6 %reshape_squeeze.55 = bf16[32,4,512]{2,1,0:T(4,128)(2,1)} reshape(bf16[1,1,32,2048]{3,2,1,0:T(8,128)(2,1)} %get-tuple-element.21) | data formatting | bytes 262144 | tf_op jit(solution)/shard_map/reshape;squeeze | solution.py:77
  32.3 1.6 %reshape_squeeze.57 = bf16[32,4,512]{2,1,0:T(4,128)(2,1)} reshape(bf16[1,1,32,2048]{3,2,1,0:T(8,128)(2,1)} %get-tuple-element.15) | data formatting | bytes 262144 | tf_op jit(solution)/shard_map/reshape;squeeze | solution.py:86
  36.3 1.6 %copy.159 = bf16[4,8,8,256]{3,2,1,0:T(8,128)(2,1)} copy(bf16[4,8,8,256]{3,1,2,0:T(8,128)(2,1)} %bitcast.298) | data formatting | bytes 262144
  40.8 3.5 %collective-permute-start.3 = (bf16[1,32,8,2,128]{4,1,2,3,0:T(8,128)(2,1)}, bf16[1,32,8,2,128]{4,1,2,3,0:T(8,128)(2,1)S(1)}, u32[]{:S(2)}, u32[]{:S(2)}) collective-permute-start(bf16[1,32,8,2,128]{4,1,2,3,0:T(8,128)(2,1)} %collective-permute-done.1), channel_id=1, source_target_pairs={{0,28},{4,0},{8,4},{12,8},{16,12},{20,16},{24,20},{28,24},{1,29},{... | collective-permute-start | bytes 393224 | tf_op jit(solution)/shard_map/ppermute | solution.py:21
  46.2 1.6 %collective-permute-done.2 = bf16[1,32,8,2,128]{4,1,2,3,0:T(8,128)(2,1)S(1)} collective-permute-done((bf16[1,32,8,2,128]{4,1,2,3,0:T(8,128)(2,1)}, bf16[1,32,8,2,128]{4,1,2,3,0:T(8,128)(2,1)S(1)}, u32[]{:S(2)}, u32[]{:S(2)}) %collective-permute-start.2) | collective-permute-done | bytes 131104 | tf_op jit(solution)/shard_map/ppermute | solution.py:16
  48.0 3.6 %collective-permute-start.5 = (bf16[1,32,8,2,128]{4,1,2,3,0:T(8,128)(2,1)S(1)}, bf16[1,32,8,2,128]{4,1,2,3,0:T(8,128)(2,1)S(1)}, u32[]{:S(2)}, u32[]{:S(2)}) collective-permute-start(bf16[1,32,8,2,128]{4,1,2,3,0:T(8,128)(2,1)S(1)} %collective-permute-done.3), channel_id=1, source_target_pairs={{0,28},{4,0},{8,4},{12,8},{16,12},{20,16},{24,20},{28,24},{1,29},{... | collective-permute-start | bytes 393224 | tf_op jit(solution)/shard_map/ppermute | solution.py:21
  51.7 2.8 %collective-permute-done.4 = bf16[1,32,8,2,128]{4,1,2,3,0:T(8,128)(2,1)S(1)} collective-permute-done((bf16[1,32,8,2,128]{4,1,2,3,0:T(8,128)(2,1)S(1)}, bf16[1,32,8,2,128]{4,1,2,3,0:T(8,128)(2,1)S(1)}, u32[]{:S(2)}, u32[]{:S(2)}) %collective-permute-start.4) | collective-permute-done | bytes 131104 | tf_op jit(solution)/shard_map/ppermute | solution.py:16
  54.5 6.1 %collective-permute-done.6 = bf16[1,32,8,2,128]{4,1,2,3,0:T(8,128)(2,1)S(1)} collective-permute-done((bf16[1,32,8,2,128]{4,1,2,3,0:T(8,128)(2,1)S(1)}, bf16[1,32,8,2,128]{4,1,2,3,0:T(8,128)(2,1)S(1)}, u32[]{:S(2)}, u32[]{:S(2)}) %collective-permute-start.6) | collective-permute-done | bytes 131104 | tf_op jit(solution)/shard_map/ppermute | solution.py:16
  63.7 2.0 %fusion.11 = bf16[64,128,16]{1,2,0:T(8,128)(2,1)} fusion(f32[64,128,16]{1,2,0:T(8,128)} %fusion.28, bf16[32,64,2,128]{3,0,1,2:T(8,128)(2,1)S(1)} %bitcast_dynamic-update-slice_fusion, s32[32]{0:T(128)S(1)} %bitcast.308, bf16[32]{0:T(256)(128)(2,1)S(1)} %get-tuple-element.5), kind=kOutput, calls=%fused_computation.23 | convolution fusion | flops 8651776 | bytes 1311744 | tf_op jit(solution)/shard_map/aqk,qsw->askw/dot_general | solution.py:46
  65.7 1.7 %squeeze.114 = bf16[64,2,1024]{2,1,0:T(2,128)(2,1)} reshape(bf16[1,64,16,128]{3,2,1,0:T(8,128)(2,1)} %bitcast.266) | data formatting | bytes 524288 | tf_op jit(solution)/shard_map/squeeze | solution.py:80
  67.4 1.8 %squeeze.119 = bf16[64,4,512]{2,1,0:T(4,128)(2,1)} reshape(bf16[1,64,16,128]{3,2,1,0:T(8,128)(2,1)} %bitcast.267) | data formatting | bytes 524288 | tf_op jit(solution)/shard_map/squeeze | solution.py:80
  75.6 1.9 %fusion.80 = f32[4,64,512]{2,1,0:T(8,128)} fusion(bf16[32,4,512]{2,1,0:T(4,128)(2,1)S(1)} %copy-done.11, bf16[64,2,4,32]{0,3,2,1:T(8,128)(2,1)} %bitcast.292), kind=kOutput, calls=%fused_computation.124 | convolution fusion | flops 8388608 | bytes 688128 | tf_op jit(solution)/shard_map/rgm,sgr->sgm/dot_general | solution.py:31
  86.3 8.9 %all_gather.3 = bf16[1,4,64,2,32]{2,4,3,0,1:T(8,128)(2,1)S(1)} all-gather(bf16[1,1,64,2,32]{2,4,3,0,1:T(8,128)(2,1)S(1)} %maximum_bitcast_fusion), channel_id=1, replica_groups=mesh['ang'=8,'row'=4] {'row'}, dimensions={1}, use_global_device_ids=true | all-gather | bytes 40960 | tf_op jit(solution)/shard_map/all_gather | solution.py:138
  108.5 1.6 %subtract_bitcast_fusion = (f32[64,1,2048]{2,0,1:T(8,128)S(1)}, f32[64,1,2048]{2,0,1:T(8,128)S(1)}) fusion(f32[64,2048]{1,0:T(8,128)S(1)} %fusion, f32[]{:T(128)} %bitcast.69, f32[]{:T(128)} %bitcast, f32[64,2048]{1,0:T(8,128)S(1)} %fusion.64, bf16[64,32]{0,1:T(8,128)(2,1)S(1)} %fusion.23, bf16[1,2,32,2048]{3,2,1,0:T(8,128)(2,1)S(1)} %copy-done.2, ...), kind=kOutput, calls=%fused_computation.56 | convolution fusion | flops 9830400 | bytes 4333576 | tf_op jit(solution)/shard_map/rm,sr->sm/dot_general | solution.py:31
  111.2 29.8 %reduce-scatter.2.cloned.1.call-done = f32[8,2,2048]{2,0,1:T(8,128)} async-done(((f32[64,2,2048]{2,0,1:T(8,128)}), f32[8,2,2048]{2,0,1:T(8,128)}) %reduce-scatter.2.cloned.1.call-update) | async-done | bytes 131088 | tf_op jit(solution)/shard_map/reduce_scatter | solution.py:168
  141.0 1.7 %copy.146 = f32[8,2,2048]{2,1,0:T(2,128)} copy(f32[8,2,2048]{2,0,1:T(8,128)} %reduce-scatter.2.cloned.1.call-done) | data formatting | bytes 262144 | tf_op jit(solution)/shard_map/reduce_scatter | solution.py:168
  (168 shorter events, 46.9 us)
Async XLA Ops:
  6.5 6.2 %copy-start = (f32[8,2]{0,1:T(2,128)S(1)}, f32[8,2]{0,1:T(2,128)}, u32[]{:S(2)}) copy-start(f32[8,2]{0,1:T(2,128)} %param.15) | copy-start | bytes 196
  6.5 10.8 %copy-start.14 = (bf16[1,3,2,32,2048]{4,3,2,1,0:T(8,128)(2,1)S(1)}, bf16[1,3,2,32,2048]{4,3,2,1,0:T(8,128)(2,1)}, u32[]{:S(2)}) copy-start(bf16[1,3,2,32,2048]{4,3,2,1,0:T(8,128)(2,1)} %param.17) | copy-start | bytes 2359300
  6.5 134.4 %reduce-scatter.2.cloned.1.call-start = ((), (), s32[]{:S(2)}) async-start(), calls=%async_computation.1 | async-start | bytes 1179648 | tf_op jit(solution)/shard_map/reduce_scatter | solution.py:168
  8.2 32.5 %collective-permute-start = (bf16[1,32,8,2,128]{4,1,2,3,0:T(8,128)(2,1)}, bf16[1,32,8,2,128]{4,1,2,3,0:T(8,128)(2,1)}, u32[]{:S(2)}, u32[]{:S(2)}) collective-permute-start(bf16[1,32,8,2,128]{4,1,2,3,0:T(8,128)(2,1)} %copy.91), channel_id=1, source_target_pairs={{0,4},{4,8},{8,12},{12,16},{16,20},{20,24},{24,28},{28,0},{1,5},{5... | collective-permute-start | bytes 393224 | tf_op jit(solution)/shard_map/ppermute | solution.py:16
  8.7 32.1 %collective-permute-start.1 = (bf16[1,32,8,2,128]{4,1,2,3,0:T(8,128)(2,1)}, bf16[1,32,8,2,128]{4,1,2,3,0:T(8,128)(2,1)}, u32[]{:S(2)}, u32[]{:S(2)}) collective-permute-start(bf16[1,32,8,2,128]{4,1,2,3,0:T(8,128)(2,1)} %copy.91), channel_id=1, source_target_pairs={{0,28},{4,0},{8,4},{12,8},{16,12},{20,16},{24,20},{28,24},{1,29},{... | collective-permute-start | bytes 393224 | tf_op jit(solution)/shard_map/ppermute | solution.py:21
  12.7 5.6 %copy-start.4 = (bf16[1,2,2048,256]{3,2,1,0:T(8,128)(2,1)S(1)}, bf16[1,2,2048,256]{3,2,1,0:T(8,128)(2,1)}, u32[]{:S(2)}) copy-start(bf16[1,2,2048,256]{3,2,1,0:T(8,128)(2,1)} %param.16) | copy-start | bytes 6291460
  28.3 32.3 %copy-start.33 = (s32[1,32]{1,0:T(1,128)S(1)}, s32[1,32]{1,0:T(1,128)}, u32[]{:S(2)}) copy-start(s32[1,32]{1,0:T(1,128)} %param.13) | copy-start | bytes 388
  40.8 7.0 %collective-permute-start.2 = (bf16[1,32,8,2,128]{4,1,2,3,0:T(8,128)(2,1)}, bf16[1,32,8,2,128]{4,1,2,3,0:T(8,128)(2,1)S(1)}, u32[]{:S(2)}, u32[]{:S(2)}) collective-permute-start(bf16[1,32,8,2,128]{4,1,2,3,0:T(8,128)(2,1)} %collective-permute-done), channel_id=1, source_target_pairs={{0,4},{4,8},{8,12},{12,16},{16,20},{20,24},{24,28},{28,0},{1,5},{5... | collective-permute-start | bytes 393224 | tf_op jit(solution)/shard_map/ppermute | solution.py:16
  40.8 7.3 %collective-permute-start.3 = (bf16[1,32,8,2,128]{4,1,2,3,0:T(8,128)(2,1)}, bf16[1,32,8,2,128]{4,1,2,3,0:T(8,128)(2,1)S(1)}, u32[]{:S(2)}, u32[]{:S(2)}) collective-permute-start(bf16[1,32,8,2,128]{4,1,2,3,0:T(8,128)(2,1)} %collective-permute-done.1), channel_id=1, source_target_pairs={{0,28},{4,0},{8,4},{12,8},{16,12},{20,16},{24,20},{28,24},{1,29},{... | collective-permute-start | bytes 393224 | tf_op jit(solution)/shard_map/ppermute | solution.py:21
  47.8 6.7 %collective-permute-start.4 = (bf16[1,32,8,2,128]{4,1,2,3,0:T(8,128)(2,1)S(1)}, bf16[1,32,8,2,128]{4,1,2,3,0:T(8,128)(2,1)S(1)}, u32[]{:S(2)}, u32[]{:S(2)}) collective-permute-start(bf16[1,32,8,2,128]{4,1,2,3,0:T(8,128)(2,1)S(1)} %collective-permute-done.2), channel_id=1, source_target_pairs={{0,4},{4,8},{8,12},{12,16},{16,20},{20,24},{24,28},{28,0},{1,5},{5... | collective-permute-start | bytes 393224 | tf_op jit(solution)/shard_map/ppermute | solution.py:16
  48.0 6.5 %collective-permute-start.5 = (bf16[1,32,8,2,128]{4,1,2,3,0:T(8,128)(2,1)S(1)}, bf16[1,32,8,2,128]{4,1,2,3,0:T(8,128)(2,1)S(1)}, u32[]{:S(2)}, u32[]{:S(2)}) collective-permute-start(bf16[1,32,8,2,128]{4,1,2,3,0:T(8,128)(2,1)S(1)} %collective-permute-done.3), channel_id=1, source_target_pairs={{0,28},{4,0},{8,4},{12,8},{16,12},{20,16},{24,20},{28,24},{1,29},{... | collective-permute-start | bytes 393224 | tf_op jit(solution)/shard_map/ppermute | solution.py:21
  54.4 6.2 %collective-permute-start.6 = (bf16[1,32,8,2,128]{4,1,2,3,0:T(8,128)(2,1)S(1)}, bf16[1,32,8,2,128]{4,1,2,3,0:T(8,128)(2,1)S(1)}, u32[]{:S(2)}, u32[]{:S(2)}) collective-permute-start(bf16[1,32,8,2,128]{4,1,2,3,0:T(8,128)(2,1)S(1)} %collective-permute-done.4), channel_id=1, source_target_pairs={{0,4},{4,8},{8,12},{12,16},{16,20},{20,24},{24,28},{28,0},{1,5},{5... | collective-permute-start | bytes 393224 | tf_op jit(solution)/shard_map/ppermute | solution.py:16
  65.7 5.9 %copy-start.29 = (bf16[4,8,8,256]{3,2,1,0:T(8,128)(2,1)S(1)}, bf16[4,8,8,256]{3,2,1,0:T(8,128)(2,1)}, u32[]{:S(2)}) copy-start(bf16[4,8,8,256]{3,2,1,0:T(8,128)(2,1)} %copy.157) | copy-start | bytes 393220
  74.4 7.1 %copy-start.10 = (bf16[4,8,8,256]{3,2,1,0:T(8,128)(2,1)S(1)}, bf16[4,8,8,256]{3,2,1,0:T(8,128)(2,1)}, u32[]{:S(2)}) copy-start(bf16[4,8,8,256]{3,2,1,0:T(8,128)(2,1)} %copy.159) | copy-start | bytes 393220
  75.5 9.2 %copy-start.1 = (bf16[64,128,16]{1,2,0:T(8,128)(2,1)S(1)}, bf16[64,128,16]{1,2,0:T(8,128)(2,1)}, u32[]{:S(2)}) copy-start(bf16[64,128,16]{1,2,0:T(8,128)(2,1)} %fusion.11) | copy-start | bytes 786436
  79.8 15.4 %copy-start.34 = (bf16[4]{0:T(256)(128)(2,1)S(1)}, bf16[4]{0:T(256)(128)(2,1)}, u32[]{:S(2)}) copy-start(bf16[4]{0:T(256)(128)(2,1)} %compare_convert_fusion) | copy-start | bytes 28
  81.4 15.7 %copy-start.12 = (bf16[64,2,4,2,32]{0,4,3,2,1:T(8,128)(2,1)}, bf16[64,2,4,2,32]{0,4,3,2,1:T(8,128)(2,1)S(1)}, u32[]{:S(2)}) copy-start(bf16[64,2,4,2,32]{0,4,3,2,1:T(8,128)(2,1)S(1)} %rev.8) | copy-start | bytes 196612
  81.4 13.9 %copy-start.17 = (bf16[1,1,32,4,32]{4,3,2,1,0:T(4,128)(2,1)S(1)}, bf16[1,1,32,4,32]{4,3,2,1,0:T(4,128)(2,1)}, u32[]{:S(2)}) copy-start(bf16[1,1,32,4,32]{4,3,2,1,0:T(4,128)(2,1)} %get-tuple-element.24) | copy-start | bytes 24580
  81.4 15.4 %copy-start.20 = (bf16[64,2,1024]{2,1,0:T(2,128)(2,1)S(1)}, bf16[64,2,1024]{2,1,0:T(2,128)(2,1)}, u32[]{:S(2)}) copy-start(bf16[64,2,1024]{2,1,0:T(2,128)(2,1)} %squeeze.114) | copy-start | bytes 786436
  81.5 15.4 %copy-start.26 = (bf16[32,2,1024]{2,1,0:T(2,128)(2,1)S(1)}, bf16[32,2,1024]{2,1,0:T(2,128)(2,1)}, u32[]{:S(2)}) copy-start(bf16[32,2,1024]{2,1,0:T(2,128)(2,1)} %reshape_squeeze.51) | copy-start | bytes 393220
  81.5 15.6 %copy-start.19 = (bf16[64,2,1024]{2,1,0:T(2,128)(2,1)S(1)}, bf16[64,2,1024]{2,1,0:T(2,128)(2,1)}, u32[]{:S(2)}) copy-start(bf16[64,2,1024]{2,1,0:T(2,128)(2,1)} %squeeze.112) | copy-start | bytes 786436
  82.6 14.7 %copy-start.25 = (bf16[32,2,1024]{2,1,0:T(2,128)(2,1)S(1)}, bf16[32,2,1024]{2,1,0:T(2,128)(2,1)}, u32[]{:S(2)}) copy-start(bf16[32,2,1024]{2,1,0:T(2,128)(2,1)} %reshape_squeeze.52) | copy-start | bytes 393220
  86.3 16.0 %copy-start.8 = (bf16[32,2,1024]{2,1,0:T(2,128)(2,1)S(1)}, bf16[32,2,1024]{2,1,0:T(2,128)(2,1)}, u32[]{:S(2)}) copy-start(bf16[32,2,1024]{2,1,0:T(2,128)(2,1)} %reshape_squeeze.54) | copy-start | bytes 393220
  97.5 5.9 %copy-start.16 = (bf16[64,2,2,2,32]{0,4,3,2,1:T(8,128)(2,1)S(1)}, bf16[64,2,2,2,32]{0,4,3,2,1:T(8,128)(2,1)}, u32[]{:S(2)}) copy-start(bf16[64,2,2,2,32]{0,4,3,2,1:T(8,128)(2,1)} %copy-done.15) | copy-start | bytes 98308
  (19 other events, 30.9 us)
Sparse Core Ops, SparseCore 0:
  111.3 29.6 reduce-scatter.1
